TPU v7x, 256 devices: a whole 4x4x8 slice. The times are simulated.
256 devices in a mesh: dp: 64 (over z, y, core), fsdp: 4 (over x).
Axes of the slice: x: 4, y: 4, z: 8, core: 2. Of those that a mesh axis runs over, the one named last changes fastest.
Arguments:
- feats: bfloat16 [64, 4, 8, 128, 256], P('dp', 'fsdp'), may hold values from -6 to 6
- grad_out: bfloat16 [64, 4, 8, 128, 256], P('dp', 'fsdp'), may hold values from -6 to 6
- kernel: bfloat16 [27, 256, 256], P(None, 'fsdp'), may hold values from -0.25 to 0.25
- send_bricks: int32 [64, 4, 64, 2], P('dp', 'fsdp'), may hold values from -1 to 7, as said below
- kmap: int32 [64, 4, 27, 2, 3], P('dp', 'fsdp'), may hold values from 0 to 135, as said below
- pair_count: int32 [64, 4, 27], P('dp', 'fsdp'), may hold values from 1 to 3, as said below
Outputs:
- out_feats: bfloat16 [64, 4, 8, 128, 256], P('dp', 'fsdp')
- in_grad: bfloat16 [64, 4, 8, 128, 256], P('dp', 'fsdp')
- kernel_grad: float32 [27, 256, 256], P(None, 'fsdp')
Inputs may be any that keep to these rules, and one draw needn't show every extreme that they name: `send_bricks`: entry (d, f, p, c) names the brick of device (d, f) sent to device (p, f) in slot c, or -1 for an empty slot. A device sends nothing to itself, fills exactly 48 slots, and fills both slots of at least one peer. kmap[d, f, t, 0, s] is an input brick of pool[d, f]: below 8 an own brick, else received slot p * 2 + c after the 8 own ones, and then always a slot that its sender filled. kmap[d, f, t, 1, s] is an output brick, below 8. Slots that are not live hold such ids too. `pair_count`: on some device every offset has 3 live slots.
All inputs are finite; a program needn't handle non-finite values.
Results may differ from a plain program's by a relative error of at most 0.0046.
Values may be sent and summed in bfloat16 or wider, within the bound.
No kernel may reach another device: no remote copies, remote signals or barrier semaphores. Data moves between devices by JAX's collectives and lax.ppermute only.
A program may use at most 192 MiB of HBM per device.

v0:
```python
import jax
import jax.numpy as jnp
from jax import lax
from jax.sharding import PartitionSpec as P


def on_device(feats, grad_out, kernel, send_bricks, kmap, pair_count):
    own_rows = feats[0, 0]
    upstream_rows = grad_out[0, 0]
    senders = send_bricks[0, 0]
    peer_total = senders.shape[0]
    slot_cap = senders.shape[1]
    brick_total = own_rows.shape[0]
    brick_rows = own_rows.shape[1]
    channels = own_rows.shape[2]
    filled = senders >= 0
    outgoing = own_rows[jnp.maximum(senders, 0)] * filled[:, :, None, None].astype(jnp.bfloat16)
    incoming = lax.all_to_all(outgoing, "dp", split_axis=0, concat_axis=0, tiled=True)
    weights = lax.all_gather(kernel, "fsdp", axis=1, tiled=True)
    pool = jnp.concatenate(
        [own_rows, incoming.reshape(peer_total * slot_cap, brick_rows, channels)], axis=0
    )
    pool_total = pool.shape[0]
    source_map = kmap[0, 0, :, 0, :]
    target_map = kmap[0, 0, :, 1, :]
    counts = pair_count[0, 0]
    tap_total = source_map.shape[0]
    slot_total = source_map.shape[1]
    active = (jnp.arange(slot_total)[None, :] < counts[:, None]).astype(jnp.bfloat16)
    inputs = pool[source_map] * active[:, :, None, None]
    upstream = upstream_rows[target_map] * active[:, :, None, None]
    contrib = jnp.einsum("tsvc,tcd->tsvd", inputs, weights, preferred_element_type=jnp.float32)
    produced = jax.ops.segment_sum(
        contrib.reshape(tap_total * slot_total, brick_rows, channels),
        target_map.reshape(-1),
        num_segments=brick_total,
    )
    backward = jnp.einsum("tsvd,tcd->tsvc", upstream, weights, preferred_element_type=jnp.float32)
    pool_grad = jax.ops.segment_sum(
        backward.reshape(tap_total * slot_total, brick_rows, channels),
        source_map.reshape(-1),
        num_segments=pool_total,
    )
    partial_value = jnp.einsum(
        "tsvc,tsvd->tcd", inputs, upstream, preferred_element_type=jnp.float32
    )
    ghosts = (
        pool_grad[brick_total:]
        .astype(jnp.bfloat16)
        .reshape(peer_total, slot_cap, brick_rows, channels)
    )
    returned = lax.all_to_all(ghosts, "dp", split_axis=0, concat_axis=0, tiled=True)
    owners = jnp.where(filled, senders, brick_total).reshape(-1)
    gathered_back = jax.ops.segment_sum(
        returned.reshape(peer_total * slot_cap, brick_rows, channels).astype(jnp.float32),
        owners,
        num_segments=brick_total + 1,
    )[:brick_total]
    in_grad = (pool_grad[:brick_total] + gathered_back).astype(jnp.bfloat16)
    divisor = jnp.float32(4 * lax.axis_size("dp") * lax.axis_size("fsdp"))
    shard_width = kernel.shape[1]
    summed = lax.psum(partial_value, ("dp", "fsdp"))
    portion = lax.dynamic_slice_in_dim(summed, lax.axis_index("fsdp") * shard_width, shard_width, 1)
    kernel_grad = portion / divisor
    return (produced.astype(jnp.bfloat16)[None, None], in_grad[None, None], kernel_grad)


def solution(mesh):
    placed = (
        P("dp", "fsdp", None, None, None),
        P("dp", "fsdp", None, None, None),
        P(None, "fsdp", None),
        P("dp", "fsdp", None, None),
        P("dp", "fsdp", None, None, None),
        P("dp", "fsdp", None),
    )
    return jax.shard_map(
        on_device,
        mesh=mesh,
        in_specs=placed,
        out_specs=(
            P("dp", "fsdp", None, None, None),
            P("dp", "fsdp", None, None, None),
            P(None, "fsdp", None),
        ),
        check_vma=False,
    )
```

profile of v0, /device:TPU:2, one launch (start us, length us, event | category | flops | bytes accessed | tf_op | source)
XLA Modules:
  0.0 672.3 jit_solution(8817993394391642369)
XLA Ops:
  8.0 0.0 copy-start
  8.0 0.7 fusion.20
  8.8 0.7 broadcast_maximum_fusion
  9.4 0.1 copy.22
  9.5 0.1 copy.21
  9.6 0.1 reshape.152
  9.8 7.5 %gather_fusion = bf16[128,128,256]{2,1,0:T(8,128)(2,1)} fusion(bf16[8,128,256]{2,1,0:T(8,128)(2,1)} %bitcast.48, s32[1024]{0:T(1024)S(1)} %pad_clamp_fusion.2), kind=kCustom, calls=%fused_computation | custom fusion | bytes 16777728 | tf_op jit(solution)/shard_map/gather | solution.py:17
  17.3 7.3 %broadcast_multiply_fusion = bf16[64,2,128,256]{3,2,1,0:T(8,128)(2,1)} fusion(bf16[64,2,128,256]{3,2,1,0:T(8,128)(2,1)} %bitcast.52, bf16[64,2]{1,0:T(8,128)(2,1)S(1)} %copy.22), kind=kLoop, calls=%fused_computation.16 | loop fusion | flops 4194304 | bytes 16777472 | tf_op jit(solution)/shard_map/mul | solution.py:17
  24.6 0.0 copy-start.3
  24.6 12.5 %all-to-all-start = ((bf16[64,2,128,256]{3,2,1,0:T(8,128)(2,1)}), bf16[64,2,128,256]{3,2,1,0:T(8,128)(2,1)}, u32[]{:S(2)}, u32[]{:S(2)}) async-start(bf16[64,2,128,256]{3,2,1,0:T(8,128)(2,1)} %broadcast_multiply_fusion), calls=%async_computation | async-start | bytes 16777216 | tf_op jit(solution)/shard_map/all_to_all | solution.py:18
  37.1 0.0 all-gather.2.cloned.1.call-start
  37.1 0.7 all-gather.2.cloned.1.call-update
  37.8 0.0 copy-done.3
  37.8 0.1 copy.27
  37.9 0.1 reshape.168
  38.0 0.1 copy.26
  38.1 0.1 reshape.184
  38.3 0.0 copy-done
  38.3 5.6 gather_fusion.2
  43.9 0.0 copy-start.5
  43.9 8.0 %copy.28 = bf16[27,3,128,256]{2,3,1,0:T(8,128)(2,1)} copy(bf16[27,3,128,256]{3,2,1,0:T(8,128)(2,1)} %bitcast.55) | data formatting | bytes 10616832 | tf_op jit(solution)/shard_map/gather | solution.py:31
  51.9 0.0 copy-done.5
  51.9 0.1 fusion.19
  52.0 33.4 %all-gather.2.cloned.1.call-done = bf16[27,256,256]{2,1,0:T(8,128)(2,1)} async-done(((bf16[27,64,256]{2,1,0:T(8,128)(2,1)}), bf16[27,256,256]{2,1,0:T(8,128)(2,1)}) %all-gather.2.cloned.1.call-update) | async-done | bytes 3538960 | tf_op jit(solution)/shard_map/all_gather | solution.py:19
  85.4 9.4 %fusion.2 = f32[27,3,128,256]{3,2,1,0:T(8,128)} fusion(bf16[27,3,128,256]{2,3,1,0:T(8,128)(2,1)} %copy.28, bf16[27,256,256]{2,1,0:T(8,128)(2,1)} %all-gather.2.cloned.1.call-done, bf16[27,3]{1,0:T(8,128)(2,1)S(1)} %fusion.19), kind=kOutput, calls=%fused_computation.11 | convolution fusion | flops 1361608704 | bytes 19464354 | tf_op jit(solution)/shard_map/tsvd,tcd->tsvc/dot_general | solution.py:38
  94.8 8.4 %broadcast_in_dim.26 = f32[136,128,256]{2,1,0:T(8,128)} broadcast(f32[]{:T(128)} %constant.8.clone.1), dimensions={} | broadcast | bytes 17825796 | tf_op jit(solution)/shard_map/broadcast_in_dim | solution.py:39
  103.1 28.6 %scatter_fusion.1 = f32[136,128,256]{2,1,0:T(8,128)} fusion(f32[136,128,256]{2,1,0:T(8,128)} %broadcast_in_dim.26, s32[81]{0:T(128)S(1)} %reshape.184, f32[81,128,256]{2,1,0:T(8,128)} %bitcast.51), kind=kCustom, calls=%fused_computation.4 | custom fusion | flops 2654208 | bytes 31850820 | tf_op jit(solution)/shard_map/scatter-add | solution.py:39
  131.7 9.0 %slice.41 = bf16[128,128,256]{2,1,0:T(8,128)(2,1)} slice(f32[136,128,256]{2,1,0:T(8,128)} %scatter_fusion.1), slice={[8:136], [0:128], [0:256]} | slice | bytes 16777216 | tf_op jit(solution)/shard_map/slice | solution.py:48
  140.7 82.6 %all-to-all-done = bf16[64,2,128,256]{3,2,1,0:T(8,128)(2,1)} async-done(((bf16[64,2,128,256]{3,2,1,0:T(8,128)(2,1)}), bf16[64,2,128,256]{3,2,1,0:T(8,128)(2,1)}, u32[]{:S(2)}, u32[]{:S(2)}) %all-to-all-start) | async-done | bytes 8388640 | tf_op jit(solution)/shard_map/all_to_all | solution.py:18
  223.2 0.0 copy-start.2
  223.2 6.5 all-to-all-start.1
  229.8 0.2 all-reduce.2.cloned.1.call-start
  230.0 0.1 copy.23
  230.1 0.1 reshape.160
  230.2 0.0 copy-done.2
  230.2 7.6 %pad_maximum_fusion = bf16[136,128,256]{2,1,0:T(8,128)(2,1)} fusion(bf16[128,128,256]{2,1,0:T(8,128)(2,1)} %bitcast.3, bf16[8,128,256]{2,1,0:T(8,128)(2,1)S(1)} %bitcast.49), kind=kLoop, calls=%fused_computation.7 | loop fusion | flops 4456448 | bytes 17825792 | tf_op jit(solution)/shard_map/concatenate | solution.py:20
  237.9 9.2 %gather_fusion.1 = bf16[81,128,256]{2,1,0:T(8,128)(2,1)} fusion(bf16[136,128,256]{2,1,0:T(8,128)(2,1)} %pad_maximum_fusion, s32[1024]{0:T(1024)S(1)} %pad_clamp_fusion.1), kind=kCustom, calls=%fused_computation.1 | custom fusion | bytes 10617156 | tf_op jit(solution)/shard_map/gather | solution.py:30
  247.0 8.0 %copy.24 = bf16[27,3,128,256]{2,3,1,0:T(8,128)(2,1)} copy(bf16[27,3,128,256]{3,2,1,0:T(8,128)(2,1)} %bitcast.54) | data formatting | bytes 10616832 | tf_op jit(solution)/shard_map/gather | solution.py:30
  255.1 9.0 %fusion.9 = f32[27,256,256]{2,1,0:T(8,128)} fusion(bf16[27,3,128,256]{2,3,1,0:T(8,128)(2,1)} %copy.28, bf16[27,3,128,256]{2,3,1,0:T(8,128)(2,1)} %copy.24, bf16[27,3]{1,0:T(8,128)(2,1)S(1)} %fusion.19), kind=kOutput, calls=%fused_computation.19 | convolution fusion | flops 1364262912 | bytes 17694882 | tf_op jit(solution)/shard_map/tsvc,tsvd->tcd/dot_general | solution.py:44
  264.1 0.0 copy-start.4
  264.1 0.0 all-reduce.2.cloned.1.call-update
  264.1 0.6 copy-done.4
  264.8 0.1 copy.30
  264.9 0.1 copy.20
  265.0 0.1 reshape.176
  265.1 0.1 squeeze.19
  265.2 9.4 %fusion.5 = f32[27,3,128,256]{3,2,1,0:T(8,128)} fusion(bf16[27,3,128,256]{2,3,1,0:T(8,128)(2,1)} %copy.24, bf16[27,256,256]{2,1,0:T(8,128)(2,1)} %all-gather.2.cloned.1.call-done, bf16[27,3]{1,0:T(8,128)(2,1)S(1)} %fusion.19), kind=kOutput, calls=%fused_computation.14 | convolution fusion | flops 1361608704 | bytes 19464354 | tf_op jit(solution)/shard_map/tsvc,tcd->tsvd/dot_general | solution.py:32
  274.6 0.1 broadcast_in_dim.12
  274.7 18.1 %scatter_fusion = f32[8,128,256]{2,1,0:T(8,128)S(1)} fusion(f32[8,128,256]{2,1,0:T(8,128)S(1)} %broadcast_in_dim.12, s32[81]{0:T(128)S(1)} %reshape.176, f32[81,128,256]{2,1,0:T(8,128)} %bitcast.50), kind=kCustom, calls=%fused_computation.3 | custom fusion | flops 2654208 | bytes 31850820 | tf_op jit(solution)/shard_map/scatter-add | solution.py:33
  292.7 0.8 convert_bitcast_fusion
  293.6 330.5 %all-reduce.2.cloned.1.call-done = f32[27,256,256]{2,1,0:T(8,128)} async-done(((f32[27,256,256]{2,1,0:T(8,128)}), f32[27,256,256]{2,1,0:T(8,128)}) %all-reduce.2.cloned.1.call-update) | async-done | bytes 7077904 | tf_op jit(solution)/shard_map/psum | solution.py:62
  624.1 2.9 dynamic-slice_multiply_fusion
  627.0 0.0 all-to-all-done.1
  627.0 11.5 %bitcast_convert_fusion = f32[128,128,256]{2,1,0:T(8,128)} fusion(bf16[64,2,128,256]{3,2,1,0:T(8,128)(2,1)} %all-to-all-done.1), kind=kLoop, calls=%fused_computation.8 | loop fusion | flops 4194304 | bytes 25165824 | tf_op jit(solution)/shard_map/convert_element_type | solution.py:55
  638.5 0.1 broadcast_in_dim.27
  638.6 0.0 copy-start.1
  638.6 24.1 %scatter_fusion.2 = f32[9,128,256]{2,1,0:T(8,128)S(1)} fusion(f32[9,128,256]{2,1,0:T(8,128)S(1)} %broadcast_in_dim.27, s32[128]{0:T(128)S(1)} %fusion.21, f32[128,128,256]{2,1,0:T(8,128)} %bitcast_convert_fusion), kind=kCustom, calls=%fused_computation.5 | custom fusion | flops 4194304 | bytes 50332160 | tf_op jit(solution)/shard_map/scatter-add | solution.py:54
  662.7 2.1 fusion.18
  664.8 0.0 copy-done.1
  (6 shorter events, 0.0 us)
Async XLA Ops:
  8.0 30.3 %copy-start = (bf16[1,1,8,128,256]{4,3,2,1,0:T(8,128)(2,1)S(1)}, bf16[1,1,8,128,256]{4,3,2,1,0:T(8,128)(2,1)}, u32[]{:S(2)}) copy-start(bf16[1,1,8,128,256]{4,3,2,1,0:T(8,128)(2,1)} %param.7) | copy-start | bytes 1572868
  24.6 13.2 %copy-start.3 = (s32[1,1,27,2,3]{2,3,4,1,0:T(2,128)S(1)}, s32[1,1,27,2,3]{2,3,4,1,0:T(2,128)}, u32[]{:S(2)}) copy-start(s32[1,1,27,2,3]{2,3,4,1,0:T(2,128)} %param.10) | copy-start | bytes 1948
  24.6 198.7 %all-to-all-start = ((bf16[64,2,128,256]{3,2,1,0:T(8,128)(2,1)}), bf16[64,2,128,256]{3,2,1,0:T(8,128)(2,1)}, u32[]{:S(2)}, u32[]{:S(2)}) async-start(bf16[64,2,128,256]{3,2,1,0:T(8,128)(2,1)} %broadcast_multiply_fusion), calls=%async_computation | async-start | bytes 16777216 | tf_op jit(solution)/shard_map/all_to_all | solution.py:18
  37.1 48.3 %all-gather.2.cloned.1.call-start = ((), (), s32[]{:S(2)}) async-start(), calls=%async_computation.2 | async-start | bytes 4423680 | tf_op jit(solution)/shard_map/all_gather | solution.py:19
  43.9 8.0 %copy-start.5 = (s32[1,1,27]{2,1,0:T(1,128)S(1)}, s32[1,1,27]{2,1,0:T(1,128)}, u32[]{:S(2)}) copy-start(s32[1,1,27]{2,1,0:T(1,128)} %param.11) | copy-start | bytes 328
  223.2 7.0 %copy-start.2 = (bf16[1,1,8,128,256]{4,3,2,1,0:T(8,128)(2,1)S(1)}, bf16[1,1,8,128,256]{4,3,2,1,0:T(8,128)(2,1)}, u32[]{:S(2)}) copy-start(bf16[1,1,8,128,256]{4,3,2,1,0:T(8,128)(2,1)} %param.6) | copy-start | bytes 1572868
  223.2 403.7 %all-to-all-start.1 = ((bf16[64,2,128,256]{3,2,1,0:T(8,128)(2,1)}), bf16[64,2,128,256]{3,2,1,0:T(8,128)(2,1)}, u32[]{:S(2)}, u32[]{:S(2)}) async-start(bf16[64,2,128,256]{3,2,1,0:T(8,128)(2,1)} %bitcast.53), calls=%async_computation.1 | async-start | bytes 16777216 | tf_op jit(solution)/shard_map/all_to_all | solution.py:52
  229.8 394.3 %all-reduce.2.cloned.1.call-start = ((), (), s32[]{:S(2)}) async-start(), calls=%async_computation.3 | async-start | bytes 14155776 | tf_op jit(solution)/shard_map/psum | solution.py:62
  264.1 0.7 copy-start.4
  638.6 26.3 %copy-start.1 = (bf16[1,1,8,128,256]{4,3,2,1,0:T(8,128)(2,1)S(1)}, bf16[1,1,8,128,256]{4,3,2,1,0:T(8,128)(2,1)}, u32[]{:S(2)}) copy-start(bf16[1,1,8,128,256]{4,3,2,1,0:T(8,128)(2,1)} %param.7) | copy-start | bytes 1572868
Sparse Core Ops, SparseCore 0:
  39.7 45.6 all-gather.1
Sparse Core Ops, SparseCore 1:
  264.2 359.9 all-reduce.1
where the time goes:
time: 674 us; the launch traced here: 672 us
  waiting for transfers between devices  447 us (66%)
  other arithmetic  105 us (16%)
  local copies, waits for them, and re-layouts  57.9 us (9%)
  matrix products  27.7 us (4%)
  starting transfers between devices  19.3 us (3%)
  between operations  15.6 us (2%)
    psum x1, waiting for transfers between devices, on_device(): summed = lax.psum(partial_value, ('dp', 'fsdp'))  331 us
    all_to_all x1, waiting for transfers between devices, on_device(): lax.all_to_all(outgoing, 'dp', split_axis=0, concat_axis=0, tiled=True)  82.6 us
    all_gather x1, waiting for transfers between devices, on_device(): weights = lax.all_gather(kernel, 'fsdp', axis=1, tiled=True)  33.4 us
    scatter-add x1, other arithmetic, on_device(): jax.ops.segment_sum(backward.reshape(tap_total * slot_total, brick_rows,...  28.6 us
    scatter-add x1, other arithmetic, on_device(): jax.ops.segment_sum(returned.reshape(peer_total * slot_cap, brick_rows, c...  24.1 us
    scatter-add x1, other arithmetic, on_device(): jax.ops.segment_sum(contrib.reshape(tap_total * slot_total, brick_rows, c...  18.1 us
    gather x2, local copies, waits for them, and re-layouts, on_device(): inputs = pool[source_map] * active[:, :, None, None]  17.2 us
    gather x2, local copies, waits for them, and re-layouts, on_device(): upstream = upstream_rows[target_map] * active[:, :, None, None]  13.6 us
  transfers between devices with their start and end apart: 4, of which 3 were waited for; matrix products, arithmetic and copies ran while one was open for 20% of the time, Pallas kernels for 0%

commit v1 on v0

--- a/solution.py
+++ b/solution.py
@@ -2,6 +2,22 @@
 import jax.numpy as jnp
 from jax import lax
 from jax.sharding import PartitionSpec as P
+
+
+def collect(x, axis, dim):
+    ways, here, step = (lax.axis_size(axis), lax.axis_index(axis), x.shape[dim])
+    lengths = [n * ways if d == dim else n for d, n in enumerate(x.shape)]
+    full = lax.dynamic_update_slice_in_dim(jnp.zeros(lengths, x.dtype), x, here * step, axis=dim)
+    going_up = going_down = x
+    for far in range(1, ways // 2 + 1):
+        going_up = lax.ppermute(going_up, axis, [(d, (d + 1) % ways) for d in range(ways)])
+        full = lax.dynamic_update_slice_in_dim(full, going_up, (here - far) % ways * step, axis=dim)
+        if 2 * far < ways:
+            going_down = lax.ppermute(going_down, axis, [(d, (d - 1) % ways) for d in range(ways)])
+            full = lax.dynamic_update_slice_in_dim(
+                full, going_down, (here + far) % ways * step, axis=dim
+            )
+    return full
 
 
 def on_device(feats, grad_out, kernel, send_bricks, kmap, pair_count):
@@ -16,7 +32,7 @@
     filled = senders >= 0
     outgoing = own_rows[jnp.maximum(senders, 0)] * filled[:, :, None, None].astype(jnp.bfloat16)
     incoming = lax.all_to_all(outgoing, "dp", split_axis=0, concat_axis=0, tiled=True)
-    weights = lax.all_gather(kernel, "fsdp", axis=1, tiled=True)
+    weights = collect(kernel, "fsdp", 1)
     pool = jnp.concatenate(
         [own_rows, incoming.reshape(peer_total * slot_cap, brick_rows, channels)], axis=0
     )

time: 674 us -> 634 us (0.941)
  waiting for transfers between devices: 447 us -> 407 us
    psum x1, waiting for transfers between devices: 331 us -> 152 us  [on_device(): summed = lax.psum(partial_value, ('dp', 'fsdp'))]
    all_to_all x1, waiting for transfers between devices: 0.01 us -> 141 us  [on_device(): lax.all_to_all(ghosts, 'dp', split_axis=0, concat_axis=0, tiled=True)]
    all_gather x1 -> x0, waiting for transfers between devices: 33.4 us -> none  [on_device(): weights = lax.all_gather(kernel, 'fsdp', axis=1, tiled=True)]
    ppermute x0 -> x3, waiting for transfers between devices: none -> 23.8 us  [the longest x2 23.8 us: collect(): lax.ppermute(going_up, axis, [(d, (d + 1) % ways) for d in range(ways)])]
    all_to_all x1, waiting for transfers between devices: 82.6 us -> 91 us  [on_device(): lax.all_to_all(outgoing, 'dp', split_axis=0, concat_axis=0, tiled=True)]
  transfers between devices with their start and end apart: 4 -> 6, of which waited for: 3 -> 5; matrix products, arithmetic and copies ran while one was open for 20% -> 27% of each run, Pallas kernels for 0% -> 0%
where the time goes in v1:
time: 634 us; the launch traced here: 633 us
  waiting for transfers between devices  407 us (64%)
  other arithmetic  104 us (16%)
  local copies, waits for them, and re-layouts  59.9 us (9%)
  matrix products  24.3 us (4%)
  starting transfers between devices  22.9 us (4%)
  between operations  14.3 us (2%)
    psum x1, waiting for transfers between devices, on_device(): summed = lax.psum(partial_value, ('dp', 'fsdp'))  152 us
    all_to_all x1, waiting for transfers between devices, on_device(): lax.all_to_all(ghosts, 'dp', split_axis=0, concat_axis=0, tiled=True)  141 us
    all_to_all x1, waiting for transfers between devices, on_device(): lax.all_to_all(outgoing, 'dp', split_axis=0, concat_axis=0, tiled=True)  91 us
    scatter-add x1, other arithmetic, on_device(): jax.ops.segment_sum(backward.reshape(tap_total * slot_total, brick_rows,...  28.3 us
    scatter-add x1, other arithmetic, on_device(): jax.ops.segment_sum(returned.reshape(peer_total * slot_cap, brick_rows, c...  24.1 us
    ppermute x2, waiting for transfers between devices, collect(): lax.ppermute(going_up, axis, [(d, (d + 1) % ways) for d in range(ways)])  23.8 us
    scatter-add x1, other arithmetic, on_device(): jax.ops.segment_sum(contrib.reshape(tap_total * slot_total, brick_rows, c...  18.1 us
    gather x2, local copies, waits for them, and re-layouts, on_device(): inputs = pool[source_map] * active[:, :, None, None]  17.2 us
  transfers between devices with their start and end apart: 6, of which 5 were waited for; matrix products, arithmetic and copies ran while one was open for 27% of the time, Pallas kernels for 0%

profile of v1, /device:TPU:2, one launch (start us, length us, event | category | flops | bytes accessed | tf_op | source)
XLA Modules:
  0.0 632.8 jit_solution(10473587570004183911)
XLA Ops:
  7.2 0.0 copy-start
  7.2 0.7 fusion.20
  7.9 0.7 broadcast_maximum_fusion
  8.6 0.1 copy.22
  8.7 0.1 copy.21
  8.8 0.1 reshape.152
  9.0 7.5 %gather_fusion = bf16[128,128,256]{2,1,0:T(8,128)(2,1)} fusion(bf16[8,128,256]{2,1,0:T(8,128)(2,1)} %bitcast.48, s32[1024]{0:T(1024)S(1)} %pad_clamp_fusion.2), kind=kCustom, calls=%fused_computation | custom fusion | bytes 16777728 | tf_op jit(solution)/shard_map/gather | solution.py:33
  16.4 7.3 %broadcast_multiply_fusion = bf16[64,2,128,256]{3,2,1,0:T(8,128)(2,1)} fusion(bf16[64,2,128,256]{3,2,1,0:T(8,128)(2,1)} %bitcast.52, bf16[64,2]{1,0:T(8,128)(2,1)S(1)} %copy.22), kind=kLoop, calls=%fused_computation.16 | loop fusion | flops 4194304 | bytes 16777472 | tf_op jit(solution)/shard_map/mul | solution.py:33
  23.7 12.5 %all-to-all-start = ((bf16[64,2,128,256]{3,2,1,0:T(8,128)(2,1)}), bf16[64,2,128,256]{3,2,1,0:T(8,128)(2,1)}, u32[]{:S(2)}, u32[]{:S(2)}) async-start(bf16[64,2,128,256]{3,2,1,0:T(8,128)(2,1)} %broadcast_multiply_fusion), calls=%async_computation | async-start | bytes 16777216 | tf_op jit(solution)/shard_map/all_to_all | solution.py:34
  36.2 0.0 copy-done.5
  36.2 1.6 collective-permute-start
  37.8 0.5 collective-permute-start.1
  38.4 0.1 copy.27
  38.5 0.1 reshape.168
  38.6 19.2 %collective-permute-done = bf16[27,64,256]{2,1,0:T(8,128)(2,1)S(1)} collective-permute-done((bf16[27,64,256]{2,1,0:T(8,128)(2,1)S(1)}, bf16[27,64,256]{2,1,0:T(8,128)(2,1)S(1)}, u32[]{:S(2)}, u32[]{:S(2)}) %collective-permute-start) | collective-permute-done | bytes 884768 | tf_op jit(solution)/shard_map/ppermute | solution.py:13
  57.8 1.5 collective-permute-start.2
  59.4 0.1 copy.26
  59.5 0.1 reshape.184
  59.6 5.6 gather_fusion.2
  65.2 8.0 %copy.28 = bf16[27,3,128,256]{2,3,1,0:T(8,128)(2,1)} copy(bf16[27,3,128,256]{3,2,1,0:T(8,128)(2,1)} %bitcast.55) | data formatting | bytes 10616832 | tf_op jit(solution)/shard_map/gather | solution.py:47
  73.2 0.4 broadcast_in_dim.28
  73.6 0.1 constant_dynamic-update-slice_fusion.3
  73.7 0.1 copy-done.8
  73.8 0.1 fusion.19
  73.9 0.1 constant_dynamic-update-slice_fusion.2
  74.0 0.0 collective-permute-done.1
  74.0 0.1 constant_dynamic-update-slice_fusion.1
  74.1 4.6 collective-permute-done.2
  78.7 1.2 constant_dynamic-update-slice_fusion
  79.9 0.0 copy-done.4
  80.0 0.0 copy-start.3
  80.0 5.8 fusion.2
  85.8 0.0 copy-done.3
  85.8 8.3 %broadcast_in_dim.30 = f32[136,128,256]{2,1,0:T(8,128)} broadcast(f32[]{:T(128)} %constant.20.clone.1), dimensions={} | broadcast | bytes 17825796 | tf_op jit(solution)/shard_map/broadcast_in_dim | solution.py:55
  94.1 28.3 %scatter_fusion.1 = f32[136,128,256]{2,1,0:T(8,128)} fusion(f32[136,128,256]{2,1,0:T(8,128)} %broadcast_in_dim.30, s32[81]{0:T(128)S(1)} %reshape.184, f32[81,128,256]{2,1,0:T(8,128)} %bitcast.51), kind=kCustom, calls=%fused_computation.4 | custom fusion | flops 2654208 | bytes 31850820 | tf_op jit(solution)/shard_map/scatter-add | solution.py:55
  122.4 9.0 %slice.41 = bf16[128,128,256]{2,1,0:T(8,128)(2,1)} slice(f32[136,128,256]{2,1,0:T(8,128)} %scatter_fusion.1), slice={[8:136], [0:128], [0:256]} | slice | bytes 16777216 | tf_op jit(solution)/shard_map/slice | solution.py:64
  131.4 91.0 %all-to-all-done = bf16[64,2,128,256]{3,2,1,0:T(8,128)(2,1)} async-done(((bf16[64,2,128,256]{3,2,1,0:T(8,128)(2,1)}), bf16[64,2,128,256]{3,2,1,0:T(8,128)(2,1)}, u32[]{:S(2)}, u32[]{:S(2)}) %all-to-all-start) | async-done | bytes 8388640 | tf_op jit(solution)/shard_map/all_to_all | solution.py:34
  222.4 6.5 %all-to-all-start.1 = ((bf16[64,2,128,256]{3,2,1,0:T(8,128)(2,1)}), bf16[64,2,128,256]{3,2,1,0:T(8,128)(2,1)}, u32[]{:S(2)}, u32[]{:S(2)}) async-start(bf16[64,2,128,256]{3,2,1,0:T(8,128)(2,1)} %bitcast.53), calls=%async_computation.1 | async-start | bytes 16777216 | tf_op jit(solution)/shard_map/all_to_all | solution.py:68
  228.9 0.3 all-reduce.2.cloned.1.call-start
  229.2 0.1 copy.23
  229.3 0.1 reshape.160
  229.4 0.0 copy-done.2
  229.4 7.6 %pad_maximum_fusion = bf16[136,128,256]{2,1,0:T(8,128)(2,1)} fusion(bf16[128,128,256]{2,1,0:T(8,128)(2,1)} %bitcast.3, bf16[8,128,256]{2,1,0:T(8,128)(2,1)S(1)} %bitcast.49), kind=kLoop, calls=%fused_computation.7 | loop fusion | flops 4456448 | bytes 17825792 | tf_op jit(solution)/shard_map/concatenate | solution.py:36
  237.0 9.2 %gather_fusion.1 = bf16[81,128,256]{2,1,0:T(8,128)(2,1)} fusion(bf16[136,128,256]{2,1,0:T(8,128)(2,1)} %pad_maximum_fusion, s32[1024]{0:T(1024)S(1)} %pad_clamp_fusion.1), kind=kCustom, calls=%fused_computation.1 | custom fusion | bytes 10617156 | tf_op jit(solution)/shard_map/gather | solution.py:46
  246.2 8.0 %copy.24 = bf16[27,3,128,256]{2,3,1,0:T(8,128)(2,1)} copy(bf16[27,3,128,256]{3,2,1,0:T(8,128)(2,1)} %bitcast.54) | data formatting | bytes 10616832 | tf_op jit(solution)/shard_map/gather | solution.py:46
  254.3 9.1 %fusion.9 = f32[27,256,256]{2,1,0:T(8,128)} fusion(bf16[27,3,128,256]{2,3,1,0:T(8,128)(2,1)} %copy.28, bf16[27,3,128,256]{2,3,1,0:T(8,128)(2,1)} %copy.24, bf16[27,3]{1,0:T(8,128)(2,1)S(1)} %fusion.19), kind=kOutput, calls=%fused_computation.19 | convolution fusion | flops 1364262912 | bytes 17694882 | tf_op jit(solution)/shard_map/tsvc,tsvd->tcd/dot_general | solution.py:60
  263.4 0.0 all-reduce.2.cloned.1.call-update
  263.4 0.7 copy-done.7
  264.1 0.1 copy.30
  264.2 0.1 copy.20
  264.3 0.1 reshape.176
  264.4 0.1 squeeze.19
  264.5 9.4 %fusion.5 = f32[27,3,128,256]{3,2,1,0:T(8,128)} fusion(bf16[27,3,128,256]{2,3,1,0:T(8,128)(2,1)} %copy.24, bf16[27,256,256]{2,1,0:T(8,128)(2,1)} %copy-done.3, bf16[27,3]{1,0:T(8,128)(2,1)S(1)} %fusion.19), kind=kOutput, calls=%fused_computation.14 | convolution fusion | flops 1361608704 | bytes 19464354 | tf_op jit(solution)/shard_map/tsvc,tcd->tsvd/dot_general | solution.py:48
  273.9 0.1 broadcast_in_dim.14
  274.0 18.1 %scatter_fusion = f32[8,128,256]{2,1,0:T(8,128)S(1)} fusion(f32[8,128,256]{2,1,0:T(8,128)S(1)} %broadcast_in_dim.14, s32[81]{0:T(128)S(1)} %reshape.176, f32[81,128,256]{2,1,0:T(8,128)} %bitcast.50), kind=kCustom, calls=%fused_computation.3 | custom fusion | flops 2654208 | bytes 31850820 | tf_op jit(solution)/shard_map/scatter-add | solution.py:49
  292.0 0.8 convert_bitcast_fusion
  292.9 140.7 %all-to-all-done.1 = bf16[64,2,128,256]{3,2,1,0:T(8,128)(2,1)} async-done(((bf16[64,2,128,256]{3,2,1,0:T(8,128)(2,1)}), bf16[64,2,128,256]{3,2,1,0:T(8,128)(2,1)}, u32[]{:S(2)}, u32[]{:S(2)}) %all-to-all-start.1) | async-done | bytes 8388640 | tf_op jit(solution)/shard_map/all_to_all | solution.py:68
  433.6 11.5 %bitcast_convert_fusion = f32[128,128,256]{2,1,0:T(8,128)} fusion(bf16[64,2,128,256]{3,2,1,0:T(8,128)(2,1)} %all-to-all-done.1), kind=kLoop, calls=%fused_computation.8 | loop fusion | flops 4194304 | bytes 25165824 | tf_op jit(solution)/shard_map/convert_element_type | solution.py:71
  445.2 0.1 broadcast_in_dim.31
  445.3 0.0 copy-start.1
  445.3 24.1 %scatter_fusion.2 = f32[9,128,256]{2,1,0:T(8,128)S(1)} fusion(f32[9,128,256]{2,1,0:T(8,128)S(1)} %broadcast_in_dim.31, s32[128]{0:T(128)S(1)} %fusion.21, f32[128,128,256]{2,1,0:T(8,128)} %bitcast_convert_fusion), kind=kCustom, calls=%fused_computation.5 | custom fusion | flops 4194304 | bytes 50332160 | tf_op jit(solution)/shard_map/scatter-add | solution.py:70
  469.4 2.1 fusion.18
  471.6 151.5 %all-reduce.2.cloned.1.call-done = f32[27,256,256]{2,1,0:T(8,128)} async-done(((f32[27,256,256]{2,1,0:T(8,128)}), f32[27,256,256]{2,1,0:T(8,128)}) %all-reduce.2.cloned.1.call-update) | async-done | bytes 7077904 | tf_op jit(solution)/shard_map/psum | solution.py:78
  623.1 2.9 dynamic-slice_multiply_fusion
  (15 shorter events, 0.0 us)
Async XLA Ops:
  7.2 52.4 %copy-start = (bf16[1,1,8,128,256]{4,3,2,1,0:T(8,128)(2,1)S(1)}, bf16[1,1,8,128,256]{4,3,2,1,0:T(8,128)(2,1)}, u32[]{:S(2)}) copy-start(bf16[1,1,8,128,256]{4,3,2,1,0:T(8,128)(2,1)} %param.7) | copy-start | bytes 1572868
  23.7 12.5 %copy-start.5 = (bf16[27,64,256]{2,1,0:T(8,128)(2,1)S(1)}, bf16[27,64,256]{2,1,0:T(8,128)(2,1)}, u32[]{:S(2)}) copy-start(bf16[27,64,256]{2,1,0:T(8,128)(2,1)} %param.8) | copy-start | bytes 2654212
  23.7 14.6 %copy-start.6 = (s32[1,1,27,2,3]{2,3,4,1,0:T(2,128)S(1)}, s32[1,1,27,2,3]{2,3,4,1,0:T(2,128)}, u32[]{:S(2)}) copy-start(s32[1,1,27,2,3]{2,3,4,1,0:T(2,128)} %param.10) | copy-start | bytes 1948
  23.7 198.7 %all-to-all-start = ((bf16[64,2,128,256]{3,2,1,0:T(8,128)(2,1)}), bf16[64,2,128,256]{3,2,1,0:T(8,128)(2,1)}, u32[]{:S(2)}, u32[]{:S(2)}) async-start(bf16[64,2,128,256]{3,2,1,0:T(8,128)(2,1)} %broadcast_multiply_fusion), calls=%async_computation | async-start | bytes 16777216 | tf_op jit(solution)/shard_map/all_to_all | solution.py:34
  36.2 21.6 %collective-permute-start = (bf16[27,64,256]{2,1,0:T(8,128)(2,1)S(1)}, bf16[27,64,256]{2,1,0:T(8,128)(2,1)S(1)}, u32[]{:S(2)}, u32[]{:S(2)}) collective-permute-start(bf16[27,64,256]{2,1,0:T(8,128)(2,1)S(1)} %copy-done.5), channel_id=1, source_target_pairs={{0,1},{1,2},{2,3},{3,0},{4,5},{5,6},{6,7},{7,4},{8,9},{9,10},{10,1... | collective-permute-start | bytes 2654216 | tf_op jit(solution)/shard_map/ppermute | solution.py:13
  37.8 36.2 %collective-permute-start.1 = (bf16[27,64,256]{2,1,0:T(8,128)(2,1)S(1)}, bf16[27,64,256]{2,1,0:T(8,128)(2,1)S(1)}, u32[]{:S(2)}, u32[]{:S(2)}) collective-permute-start(bf16[27,64,256]{2,1,0:T(8,128)(2,1)S(1)} %copy-done.5), channel_id=1, source_target_pairs={{0,3},{1,0},{2,1},{3,2},{4,7},{5,4},{6,5},{7,6},{8,11},{9,8},{10,9... | collective-permute-start | bytes 2654216 | tf_op jit(solution)/shard_map/ppermute | solution.py:16
  57.8 20.9 %collective-permute-start.2 = (bf16[27,64,256]{2,1,0:T(8,128)(2,1)S(1)}, bf16[27,64,256]{2,1,0:T(8,128)(2,1)}, u32[]{:S(2)}, u32[]{:S(2)}) collective-permute-start(bf16[27,64,256]{2,1,0:T(8,128)(2,1)S(1)} %collective-permute-done), channel_id=1, source_target_pairs={{0,1},{1,2},{2,3},{3,0},{4,5},{5,6},{6,7},{7,4},{8,9},{9,10},{10,1... | collective-permute-start | bytes 2654216 | tf_op jit(solution)/shard_map/ppermute | solution.py:13
  73.2 0.7 copy-start.8
  73.2 6.8 %copy-start.4 = (bf16[27,3,128,256]{2,3,1,0:T(8,128)(2,1)S(1)}, bf16[27,3,128,256]{2,3,1,0:T(8,128)(2,1)}, u32[]{:S(2)}) copy-start(bf16[27,3,128,256]{2,3,1,0:T(8,128)(2,1)} %copy.28) | copy-start | bytes 15925252
  80.0 5.8 copy-start.3
  222.4 7.0 %copy-start.2 = (bf16[1,1,8,128,256]{4,3,2,1,0:T(8,128)(2,1)S(1)}, bf16[1,1,8,128,256]{4,3,2,1,0:T(8,128)(2,1)}, u32[]{:S(2)}) copy-start(bf16[1,1,8,128,256]{4,3,2,1,0:T(8,128)(2,1)} %param.6) | copy-start | bytes 1572868
  222.4 211.2 %all-to-all-start.1 = ((bf16[64,2,128,256]{3,2,1,0:T(8,128)(2,1)}), bf16[64,2,128,256]{3,2,1,0:T(8,128)(2,1)}, u32[]{:S(2)}, u32[]{:S(2)}) async-start(bf16[64,2,128,256]{3,2,1,0:T(8,128)(2,1)} %bitcast.53), calls=%async_computation.1 | async-start | bytes 16777216 | tf_op jit(solution)/shard_map/all_to_all | solution.py:68
  228.9 394.2 %all-reduce.2.cloned.1.call-start = ((), (), s32[]{:S(2)}) async-start(), calls=%async_computation.2 | async-start | bytes 14155776 | tf_op jit(solution)/shard_map/psum | solution.py:78
  263.4 0.7 copy-start.7
  445.3 180.7 %copy-start.1 = (bf16[1,1,8,128,256]{4,3,2,1,0:T(8,128)(2,1)S(1)}, bf16[1,1,8,128,256]{4,3,2,1,0:T(8,128)(2,1)}, u32[]{:S(2)}) copy-start(bf16[1,1,8,128,256]{4,3,2,1,0:T(8,128)(2,1)} %param.7) | copy-start | bytes 1572868
Sparse Core Ops, SparseCore 0:
  263.5 359.4 all-reduce.1
